TPU v7x, 256 devices: a whole 4x4x8 slice. The times are simulated.
256 devices in a mesh: dp: 32 (over z, y), expert: 8 (over x, core).
Axes of the slice: x: 4, y: 4, z: 8, core: 2. Of those that a mesh axis runs over, the one named last changes fastest.
Arguments:
- residual: bfloat16 [2048, 4096], P(('dp', 'expert')), may hold values from -8.2 to 8.2
- queries: bfloat16 [2048, 4096], P('dp', 'expert'), may hold values from -24 to 24
- new_keys: bfloat16 [2048, 1024], P('dp', 'expert'), may hold values from -6 to 6
- new_values: bfloat16 [2048, 1024], P('dp', 'expert'), may hold values from -6 to 6
- cache_keys: bfloat16 [64, 1024, 1024], P('dp', None, 'expert'), may hold values from -8 to 8
- cache_values: bfloat16 [64, 1024, 1024], P('dp', None, 'expert'), may hold values from -6 to 6
- out_weight: bfloat16 [4096, 4096], P('expert', 'dp'), may hold values from -1 to 1
- ffn_gain: float32 [4096], replicated, may hold values from 0.1 to 1.9
- router: bfloat16 [4096, 8], replicated, may hold values from -0.0234375 to 0.0234375
- routes: int32 [2048, 2], P(('dp', 'expert')), may hold values from 0 to 7, all different within a row; in each aligned block of 64 rows (0 to 63, 64 to 127, ...) at most 24 rows name the same one
- w_gate: bfloat16 [8, 4096, 14336], P('expert', None, 'dp'), may hold values from -0.09375 to 0.09375
- w_up: bfloat16 [8, 4096, 14336], P('expert', None, 'dp'), may hold values from -0.09375 to 0.09375
- w_down: bfloat16 [8, 14336, 4096], P('expert', 'dp'), may hold values from -0.046875 to 0.046875
- summary_gain: float32 [4096], P('expert'), may hold values from 0.1 to 1.9
- reduce_scale: float32 [32], P('expert'), may hold values from 0.1 to 30
- assign: int32 [64], replicated, may hold values from 0 to 3
Outputs:
- summary: bfloat16 [64, 4096], P('dp', 'expert')
- reduced: bfloat16 [64, 4096], P('dp', 'expert')
Inputs may be any that keep to these rules, and one draw needn't show every extreme that they name: `routes`: each token names 2 different experts and every expert is named by some token; among the tokens of one dp index (aligned blocks of 64 rows) no expert is named by more than 24 tokens, and that bound is reached in some block.
All inputs are finite; a program needn't handle non-finite values.
Results may differ from a plain program's by a relative error of at most 0.017.
Values may be sent and summed in bfloat16 or wider, within the bound.
No kernel may reach another device: no remote copies, remote signals or barrier semaphores. Data moves between devices by JAX's collectives and lax.ppermute only.
A program may use at most 128 MiB of HBM per device.

v0:
```python
import math
import jax
import jax.numpy as jnp
from jax import lax
from jax.sharding import PartitionSpec as P

HEADS = 32
KVH = 8
HD = 128
EXPERTS = 8
WIN = 32
GROUP_CAP = 24
EPSILON = 1e-05


def attend(queries, new_keys, new_values, cache_keys, cache_values):
    span_count, cache_len, kv_width = cache_keys.shape
    kv_local = kv_width // HD
    group = HEADS // KVH
    window = queries.shape[0] // span_count
    query_view = queries.reshape(span_count, window, kv_local, group, HD)
    fresh_keys = new_keys.reshape(span_count, window, kv_local, HD)
    fresh_values = new_values.reshape(span_count, window, kv_local, HD)
    stored_keys = cache_keys.reshape(span_count, cache_len, kv_local, HD)
    stored_values = cache_values.reshape(span_count, cache_len, kv_local, HD)
    factor = 1.0 / math.sqrt(HD)
    past_scores = (
        jnp.einsum("ctkgd,cpkd->ckgtp", query_view, stored_keys, preferred_element_type=jnp.float32)
        * factor
    )
    fresh_scores = (
        jnp.einsum("ctkgd,cskd->ckgts", query_view, fresh_keys, preferred_element_type=jnp.float32)
        * factor
    )
    causal = jnp.arange(window)[:, None] >= jnp.arange(window)[None, :]
    fresh_scores = jnp.where(causal, fresh_scores, -jnp.inf)
    highest = jnp.maximum(jnp.max(past_scores, axis=-1), jnp.max(fresh_scores, axis=-1))[..., None]
    past_exp = jnp.exp(past_scores - highest)
    fresh_exp = jnp.exp(fresh_scores - highest)
    totals = jnp.sum(past_exp, axis=-1, keepdims=True) + jnp.sum(fresh_exp, axis=-1, keepdims=True)
    past_weights = (past_exp / totals).astype(jnp.bfloat16)
    fresh_weights = (fresh_exp / totals).astype(jnp.bfloat16)
    context = jnp.einsum(
        "ckgtp,cpkd->ctkgd", past_weights, stored_values, preferred_element_type=jnp.float32
    )
    context = context + jnp.einsum(
        "ckgts,cskd->ctkgd", fresh_weights, fresh_values, preferred_element_type=jnp.float32
    )
    return context.astype(jnp.bfloat16).reshape(span_count * window, kv_local * group * HD)


def expert_rows(rows, w_gate, w_up, w_down):
    gate_proj = jnp.einsum("ned,edf->nef", rows, w_gate, preferred_element_type=jnp.float32)
    up_proj = jnp.einsum("ned,edf->nef", rows, w_up, preferred_element_type=jnp.float32)
    hidden = (jax.nn.silu(gate_proj) * up_proj).astype(jnp.bfloat16)
    return jnp.einsum("nef,efd->ned", hidden, w_down, preferred_element_type=jnp.float32)


def shards(
    residual,
    queries,
    new_keys,
    new_values,
    cache_keys,
    cache_values,
    out_weight,
    ffn_gain,
    router,
    routes,
    w_gate,
    w_up,
    w_down,
    summary_gain,
    reduce_scale,
    assign,
):
    expert_count = lax.axis_size("expert")
    dp_index = lax.axis_index("dp")
    column = lax.axis_index("expert")
    span_local = cache_keys.shape[0]
    tok_local = residual.shape[0]
    width = residual.shape[1]
    slice_width = width // expert_count
    highest_precision = lax.Precision.HIGHEST
    attended = attend(queries, new_keys, new_values, cache_keys, cache_values)
    head_terms = jnp.dot(
        attended,
        lax.all_gather(out_weight, "dp", axis=1, tiled=True),
        preferred_element_type=jnp.float32,
    )
    mixed = residual.astype(jnp.float32) + lax.psum_scatter(
        head_terms, "expert", scatter_dimension=0, tiled=True
    )
    normed = (
        mixed * lax.rsqrt(jnp.mean(mixed * mixed, axis=-1, keepdims=True) + EPSILON) * ffn_gain
    ).astype(jnp.bfloat16)
    logits = jnp.dot(normed, router, preferred_element_type=jnp.float32)
    expert_ids = jnp.arange(EXPERTS, dtype=jnp.int32)
    first = routes[:, 0:1] == expert_ids[None, :]
    second = routes[:, 1:2] == expert_ids[None, :]
    first_logit = jnp.sum(jnp.where(first, logits, 0.0), axis=-1)
    second_logit = jnp.sum(jnp.where(second, logits, 0.0), axis=-1)
    partner = jnp.where(first, routes[:, 1:2], jnp.where(second, routes[:, 0:1], -1))
    outgoing = jnp.where((partner >= 0).T[:, :, None], normed[None, :, :], 0)
    arrived_rows, arrived_partner = (
        lax.all_to_all(outgoing, "expert", split_axis=0, concat_axis=1, tiled=True),
        lax.all_to_all(partner.T, "expert", split_axis=0, concat_axis=1, tiled=True),
    )
    present = (arrived_partner >= 0).astype(jnp.int32)
    position = jnp.cumsum(present, axis=1) - 1
    picker = (present[:, None, :] > 0) & (
        position[:, None, :] == jnp.arange(GROUP_CAP)[None, :, None]
    )
    compact = jnp.einsum(
        "eks,esd->ked",
        picker.astype(jnp.bfloat16),
        arrived_rows,
        preferred_element_type=jnp.float32,
    ).astype(jnp.bfloat16)
    token_span = (column * tok_local + jnp.arange(tok_local)) // WIN
    pool_matrix = (token_span[None, :] == jnp.arange(span_local)[:, None]).astype(jnp.float32)
    gathered = lax.all_gather(compact, "dp", axis=0, tiled=True)
    returned = lax.psum_scatter(
        expert_rows(gathered, w_gate, w_up, w_down), "dp", scatter_dimension=0, tiled=True
    )
    spread = jnp.einsum(
        "eks,ked->esd", picker.astype(jnp.float32), returned, precision=highest_precision
    )
    back = lax.all_to_all(spread, "expert", split_axis=1, concat_axis=0, tiled=True)
    gate_table = jnp.where(first, jax.nn.sigmoid(first_logit - second_logit)[:, None], 0.0)
    gate_table = gate_table + jnp.where(
        second, jax.nn.sigmoid(second_logit - first_logit)[:, None], 0.0
    )
    token_out = mixed + jnp.einsum("te,etd->td", gate_table, back, precision=highest_precision)
    pooled_local = jnp.dot(pool_matrix, token_out, precision=highest_precision)
    pooled = lax.psum_scatter(pooled_local, "expert", scatter_dimension=1, tiled=True)
    squares = lax.psum(jnp.sum(pooled * pooled, axis=-1), "expert")
    summary = (pooled * lax.rsqrt(squares / width + EPSILON)[:, None] * summary_gain).astype(
        jnp.bfloat16
    )
    everyone = lax.all_gather(summary, "dp", axis=0, tiled=True)
    heads_local = slice_width // HD
    mine = summary.reshape(span_local, heads_local, HD)
    others = everyone.reshape(everyone.shape[0], heads_local, HD)
    factor = reduce_scale / math.sqrt(HD)
    scores = (
        jnp.einsum("chd,khd->hck", mine, others, preferred_element_type=jnp.float32)
        * factor[:, None, None]
    )
    own_assign = lax.dynamic_slice_in_dim(assign, dp_index * span_local, span_local)
    same = own_assign[:, None] == assign[None, :]
    scores = jnp.where(same[None], scores, -jnp.inf)
    highest = jnp.max(scores, axis=-1, keepdims=True)
    expo = jnp.exp(scores - highest)
    weights = (expo / jnp.sum(expo, axis=-1, keepdims=True)).astype(jnp.bfloat16)
    reduced = jnp.einsum("hck,khd->chd", weights, others, preferred_element_type=jnp.float32)
    reduced = reduced.reshape(span_local, slice_width).astype(jnp.bfloat16)
    return (summary, reduced)


def solution(mesh):
    return jax.shard_map(
        shards,
        mesh=mesh,
        in_specs=(
            P(("dp", "expert"), None),
            P("dp", "expert"),
            P("dp", "expert"),
            P("dp", "expert"),
            P("dp", None, "expert"),
            P("dp", None, "expert"),
            P("expert", "dp"),
            P(),
            P(),
            P(("dp", "expert"), None),
            P("expert", None, "dp"),
            P("expert", None, "dp"),
            P("expert", "dp", None),
            P("expert"),
            P("expert"),
            P(),
        ),
        out_specs=(P("dp", "expert"), P("dp", "expert")),
        check_vma=False,
    )
```

profile of v0, /device:TPU:8, one launch (start us, length us, event | category | flops | bytes accessed | tf_op | source)
XLA Modules:
  0.0 635.6 jit_solution(1223442760722272505)
XLA Ops:
  7.2 0.7 all-gather.4.cloned.1.call-update
  8.0 0.9 reshape.508
  9.2 1.0 fusion.83
  10.6 0.9 fusion.61
  11.5 0.4 fusion.42
  12.0 84.5 %all-gather.4.cloned.1.call-done = bf16[512,4096]{1,0:T(8,128)(2,1)} async-done(((bf16[512,128]{1,0:T(8,128)(2,1)}), bf16[512,4096]{1,0:T(8,128)(2,1)}) %all-gather.4.cloned.1.call-update) | async-done | bytes 4194320 | tf_op jit(solution)/shard_map/all_gather | solution.py:88
  96.5 4.0 fusion.58
  100.5 0.6 compare_select_fusion.1
  101.1 4.3 all-to-all-start
  105.4 30.2 %reduce-scatter.6.cloned.1.call-done = f32[8,4096]{1,0:T(8,128)} async-done(((f32[64,4096]{1,0:T(8,128)}), f32[8,4096]{1,0:T(8,128)}) %reduce-scatter.6.cloned.1.call-update) | async-done | bytes 131088 | tf_op jit(solution)/shard_map/reduce_scatter | solution.py:91
  135.5 1.1 multiply_reduce_fusion
  136.6 1.0 multiply_convert_fusion
  137.6 0.9 broadcast_select_fusion
  138.5 3.5 all-to-all-start.1
  142.5 9.8 %all-to-all-done.1 = bf16[8,8,4096]{2,1,0:T(8,128)(2,1)S(1)} async-done(((bf16[8,8,4096]{2,1,0:T(8,128)(2,1)}), bf16[8,8,4096]{2,1,0:T(8,128)(2,1)S(1)}, u32[]{:S(2)}, u32[]{:S(2)}) %all-to-all-start.1) | async-done | bytes 524320 | tf_op jit(solution)/shard_map/all_to_all | solution.py:106
  152.2 0.9 fusion.5
  153.4 86.4 %all-gather.6.cloned.1.call-done = bf16[768,1,4096]{2,0,1:T(8,128)(2,1)} async-done(((bf16[24,1,4096]{2,0,1:T(8,128)(2,1)}), bf16[768,1,4096]{2,0,1:T(8,128)(2,1)}) %all-gather.6.cloned.1.call-update) | async-done | bytes 6291472 | tf_op jit(solution)/shard_map/all_gather | solution.py:122
  239.8 6.9 %fusion.9 = f32[768,1,448]{0,2,1:T(8,128)S(1)} fusion(bf16[1,4096,448]{1,2,0:T(8,128)(2,1)} %param.26, bf16[768,1,4096]{2,0,1:T(8,128)(2,1)} %all-gather.6.cloned.1.call-done), kind=kOutput, calls=%fused_computation.13 | convolution fusion | flops 2818572288 | bytes 11337728 | tf_op jit(solution)/shard_map/ned,edf->nef/dot_general | solution.py:53
  246.7 17.8 %convolution_bitcast_fusion = f32[768,1,4096]{2,0,1:T(8,128)} fusion(bf16[1,448,4096]{2,1,0:T(8,128)(2,1)} %param.28, bf16[1,4096,448]{1,2,0:T(8,128)(2,1)} %param.27, bf16[768,1,4096]{2,0,1:T(8,128)(2,1)} %all-gather.6.cloned.1.call-done, f32[768,1,448]{0,2,1:T(8,128)S(1)} %fusion.9), kind=kOutput, calls=%fused_computation.1 | convolution fusion | flops 5639208960 | bytes 27590656 | tf_op jit(solution)/shard_map/nef,efd->ned/dot_general | solution.py:56
  264.6 236.8 %reduce-scatter.8.cloned.1.call-done = f32[24,1,4096]{2,0,1:T(8,128)} async-done(((f32[768,1,4096]{2,0,1:T(8,128)}), f32[24,1,4096]{2,0,1:T(8,128)}) %reduce-scatter.8.cloned.1.call-update) | async-done | bytes 393232 | tf_op jit(solution)/shard_map/reduce_scatter | solution.py:123
  501.4 1.6 convolution_bitcast_fusion.2
  503.0 2.1 copy.45
  505.1 4.3 all-to-all-start.2
  510.0 15.3 %all-to-all-done.2 = f32[1,64,4096]{2,0,1:T(1,128)S(1)} async-done(((f32[1,64,4096]{2,0,1:T(1,128)}), f32[1,64,4096]{2,0,1:T(1,128)S(1)}, u32[]{:S(2)}, u32[]{:S(2)}) %all-to-all-start.2) | async-done | bytes 1048608 | tf_op jit(solution)/shard_map/all_to_all | solution.py:129
  525.3 0.6 copy.86
  525.9 1.5 fusion.47
  527.4 3.2 convolution_bitcast_fusion.1
  530.7 34.0 %reduce-scatter.10.cloned.1.call-done = f32[512,2]{1,0:T(8,128)} async-done(((f32[4096,2]{1,0:T(8,128)}), f32[512,2]{1,0:T(8,128)}) %reduce-scatter.10.cloned.1.call-update) | async-done | bytes 4112
  564.6 1.1 copy.58
  565.8 12.9 %psum.7 = f32[2]{0:T(128)S(1)} all-reduce(f32[2]{0:T(128)S(1)} %multiply_reduce_fusion.1), channel_id=1, replica_groups=mesh['dp'=32,'expert'=8] {'expert'}, use_global_device_ids=true, to_apply=%region_12.13 | all-reduce | flops 2 | bytes 16 | tf_op jit(solution)/shard_map/psum | solution.py:137
  578.9 49.0 %all-gather = bf16[32,2,512]{2,1,0:T(2,128)(2,1)S(1)} all-gather(bf16[1,2,512]{2,1,0:T(2,128)(2,1)S(1)} %fusion.95), channel_id=1, replica_groups=mesh['dp'=32,'expert'=8] {'dp'}, dimensions={0}, use_global_device_ids=true | all-gather | bytes 67584 | tf_op jit(solution)/shard_map/all_gather | solution.py:141
  628.3 0.8 fusion.46
  (62 shorter events, 3.0 us)
Async XLA Ops:
  7.2 1.7 copy-start
  7.2 4.3 copy-start.8
  7.2 89.3 %all-gather.4.cloned.1.call-start = ((), (), s32[]{:S(2)}) async-start(), calls=%async_computation.6 | async-start | bytes 4325376 | tf_op jit(solution)/shard_map/all_gather | solution.py:88
  7.9 127.6 %reduce-scatter.6.cloned.1.call-start = ((), (), s32[]{:S(2)}) async-start(), calls=%async_computation.7 | async-start | bytes 1179648 | tf_op jit(solution)/shard_map/reduce_scatter | solution.py:91
  11.9 88.6 %copy-start.7 = (s32[8,2]{0,1:T(2,128)S(1)}, s32[8,2]{0,1:T(2,128)}, u32[]{:S(2)}) copy-start(s32[8,2]{0,1:T(2,128)} %param.25) | copy-start | bytes 196
  11.9 123.6 %copy-start.2 = (bf16[8,4096]{1,0:T(8,128)(2,1)S(1)}, bf16[8,4096]{1,0:T(8,128)(2,1)}, u32[]{:S(2)}) copy-start(bf16[8,4096]{1,0:T(8,128)(2,1)} %param.16) | copy-start | bytes 196612
  11.9 124.7 %copy-start.4 = (f32[4096]{0:T(1024)S(1)}, f32[4096]{0:T(1024)}, u32[]{:S(2)}) copy-start(f32[4096]{0:T(1024)} %param.23) | copy-start | bytes 49156
  101.1 37.4 %all-to-all-start = ((s32[8,1,8]{2,1,0:T(1,128)}), s32[8,1,8]{2,1,0:T(1,128)S(1)}, u32[]{:S(2)}, u32[]{:S(2)}) async-start(s32[8,1,8]{2,1,0:T(1,128)} %compare_select_fusion.1), calls=%async_computation.1 | async-start | bytes 8192 | tf_op jit(solution)/shard_map/all_to_all | solution.py:107
  138.5 13.7 %all-to-all-start.1 = ((bf16[8,8,4096]{2,1,0:T(8,128)(2,1)}), bf16[8,8,4096]{2,1,0:T(8,128)(2,1)S(1)}, u32[]{:S(2)}, u32[]{:S(2)}) async-start(bf16[8,8,4096]{2,1,0:T(8,128)(2,1)} %broadcast_select_fusion), calls=%async_computation.2 | async-start | bytes 1048576 | tf_op jit(solution)/shard_map/all_to_all | solution.py:106
  142.0 97.8 %all-gather.6.cloned.1.call-start = ((), (), s32[]{:S(2)}) async-start(), calls=%async_computation.8 | async-start | bytes 6488064 | tf_op jit(solution)/shard_map/all_gather | solution.py:122
  153.1 348.2 %reduce-scatter.8.cloned.1.call-start = ((), (), s32[]{:S(2)}) async-start(), calls=%async_computation.9 | async-start | bytes 12976128 | tf_op jit(solution)/shard_map/reduce_scatter | solution.py:123
  264.5 245.1 %copy-start.9 = (s32[64]{0:T(128)S(1)}, s32[64]{0:T(128)}, u32[]{:S(2)}) copy-start(s32[64]{0:T(128)} %param.31) | copy-start | bytes 772
  264.6 245.1 %copy-start.3 = (bf16[4096,8]{0,1:T(8,128)(2,1)S(1)}, bf16[4096,8]{0,1:T(8,128)(2,1)}, u32[]{:S(2)}) copy-start(bf16[4096,8]{0,1:T(8,128)(2,1)} %param.24) | copy-start | bytes 196612
  503.0 24.4 %copy-start.1 = (f32[8,4096]{1,0:T(8,128)S(1)}, f32[8,4096]{1,0:T(8,128)}, u32[]{:S(2)}) copy-start(f32[8,4096]{1,0:T(8,128)} %reduce-scatter.6.cloned.1.call-done) | copy-start | bytes 393220
  505.1 20.2 %all-to-all-start.2 = ((f32[1,64,4096]{2,0,1:T(1,128)}), f32[1,64,4096]{2,0,1:T(1,128)S(1)}, u32[]{:S(2)}, u32[]{:S(2)}) async-start(f32[1,64,4096]{2,0,1:T(1,128)} %copy.45), calls=%async_computation.4 | async-start | bytes 2097152 | tf_op jit(solution)/shard_map/all_to_all | solution.py:129
  509.3 55.3 %reduce-scatter.10.cloned.1.call-start = ((), (), s32[]{:S(2)}) async-start(), calls=%async_computation.10 | async-start | bytes 2359296
  510.0 55.9 %copy-start.10 = (f32[4]{0:T(128)S(1)}, f32[4]{0:T(128)}, u32[]{:S(2)}) copy-start(f32[4]{0:T(128)} %param.30) | copy-start | bytes 52
  510.0 68.8 %copy-start.5 = (f32[512]{0:T(512)S(1)}, f32[512]{0:T(512)}, u32[]{:S(2)}) copy-start(f32[512]{0:T(512)} %param.29) | copy-start | bytes 6148
  578.8 50.3 %copy-start.6 = (bf16[2,512]{1,0:T(2,128)(2,1)}, bf16[2,512]{1,0:T(2,128)(2,1)S(1)}, u32[]{:S(2)}) copy-start(bf16[2,512]{1,0:T(2,128)(2,1)S(1)} %multiply_convert_fusion.1) | copy-start | bytes 6148
Sparse Core Ops, SparseCore 0:
  10.5 85.9 all-gather.3
  100.6 34.8 reduce-scatter.5
  153.3 86.4 all-gather.5
  264.7 236.6 reduce-scatter.7
  530.7 33.8 reduce-scatter.9
where the time goes:
time: 636 us
  waiting for transfers between devices  498 us (78%)
  blocking collectives  61.9 us (10%)
  matrix products  39.8 us (6%)
  between operations  14.1 us (2%)
  starting transfers between devices  12.6 us (2%)
    reduce_scatter x1, waiting for transfers between devices, shards(): lax.psum_scatter(expert_rows(gathered, w_gate, w_up, w_down), 'dp', scatt...  237 us
    all_gather x1, waiting for transfers between devices, shards(): gathered = lax.all_gather(compact, 'dp', axis=0, tiled=True)  86.4 us
    all_gather x1, waiting for transfers between devices, shards(): lax.all_gather(out_weight, 'dp', axis=1, tiled=True)  84.5 us
    all_gather x1, blocking collectives, shards(): everyone = lax.all_gather(summary, 'dp', axis=0, tiled=True)  49 us
    unnamed x6, waiting for transfers between devices  34.7 us
    reduce_scatter x1, waiting for transfers between devices, shards(): lax.psum_scatter(head_terms, 'expert', scatter_dimension=0, tiled=True)  30.2 us
    dot_general x1, matrix products, expert_rows(): jnp.einsum('nef,efd->ned', hidden, w_down, preferred_element_type=jnp.flo...  17.8 us
    all_to_all x1, waiting for transfers between devices, shards(): lax.all_to_all(spread, 'expert', split_axis=1, concat_axis=0, tiled=True)  15.3 us
  transfers between devices with their start and end apart: 8, of which 7 were waited for; matrix products, arithmetic and copies ran while one was open for 1% of the time, Pallas kernels for 0%

commit v1 on v0

--- a/solution.py
+++ b/solution.py
@@ -138,7 +138,8 @@
     summary = (pooled * lax.rsqrt(squares / width + EPSILON)[:, None] * summary_gain).astype(
         jnp.bfloat16
     )
-    everyone = lax.all_gather(summary, "dp", axis=0, tiled=True)
+    copies = jnp.concatenate([summary] * lax.axis_size("dp"), axis=0)
+    everyone = lax.all_to_all(copies, "dp", 0, 0, tiled=True)
     heads_local = slice_width // HD
     mine = summary.reshape(span_local, heads_local, HD)
     others = everyone.reshape(everyone.shape[0], heads_local, HD)

time: 636 us -> 607 us (0.954)
  blocking collectives: 61.9 us -> 12.9 us
  starting transfers between devices: 12.6 us -> 22.8 us
  waiting for transfers between devices: 498 us -> 506 us
    all_gather x1 -> x0, blocking collectives: 49 us -> none  [shards(): everyone = lax.all_gather(summary, 'dp', axis=0, tiled=True)]
    all_to_all x0 -> x1, starting transfers between devices: none -> 10.2 us  [shards(): everyone = lax.all_to_all(copies, 'dp', 0, 0, tiled=True)]
    all_to_all x0 -> x1, waiting for transfers between devices: none -> 8.68 us  [shards(): everyone = lax.all_to_all(copies, 'dp', 0, 0, tiled=True)]
  transfers between devices with their start and end apart: 8 -> 9, of which waited for: 7 -> 8; matrix products, arithmetic and copies ran while one was open for 1% -> 1% of each run, Pallas kernels for 0% -> 0%
where the time goes in v1:
time: 607 us; the launch traced here: 606 us
  waiting for transfers between devices  506 us (83%)
  matrix products  39.8 us (7%)
  starting transfers between devices  22.8 us (4%)
  between operations  14.1 us (2%)
  blocking collectives  12.9 us (2%)
    reduce_scatter x1, waiting for transfers between devices, shards(): lax.psum_scatter(expert_rows(gathered, w_gate, w_up, w_down), 'dp', scatt...  237 us
    all_gather x1, waiting for transfers between devices, shards(): gathered = lax.all_gather(compact, 'dp', axis=0, tiled=True)  86.4 us
    all_gather x1, waiting for transfers between devices, shards(): lax.all_gather(out_weight, 'dp', axis=1, tiled=True)  84.5 us
    unnamed x6, waiting for transfers between devices  34.7 us
    reduce_scatter x1, waiting for transfers between devices, shards(): lax.psum_scatter(head_terms, 'expert', scatter_dimension=0, tiled=True)  30.2 us
    dot_general x1, matrix products, expert_rows(): jnp.einsum('nef,efd->ned', hidden, w_down, preferred_element_type=jnp.flo...  17.8 us
    all_to_all x1, waiting for transfers between devices, shards(): lax.all_to_all(spread, 'expert', split_axis=1, concat_axis=0, tiled=True)  15.4 us
    psum x1, blocking collectives, shards(): squares = lax.psum(jnp.sum(pooled * pooled, axis=-1), 'expert')  12.9 us
  transfers between devices with their start and end apart: 9, of which 8 were waited for; matrix products, arithmetic and copies ran while one was open for 1% of the time, Pallas kernels for 0%

profile of v1, /device:TPU:8, one launch (start us, length us, event | category | flops | bytes accessed | tf_op | source)
XLA Modules:
  0.0 606.4 jit_solution(2636424684395799341)
XLA Ops:
  7.2 0.7 all-gather.3.cloned.1.call-update
  8.0 0.9 reshape.511
  9.2 1.0 fusion.83
  10.6 0.9 fusion.61
  12.0 84.5 %all-gather.3.cloned.1.call-done = bf16[512,4096]{1,0:T(8,128)(2,1)} async-done(((bf16[512,128]{1,0:T(8,128)(2,1)}), bf16[512,4096]{1,0:T(8,128)(2,1)}) %all-gather.3.cloned.1.call-update) | async-done | bytes 4194320 | tf_op jit(solution)/shard_map/all_gather | solution.py:88
  96.5 4.0 fusion.58
  101.1 4.3 all-to-all-start
  105.4 30.2 %reduce-scatter.6.cloned.1.call-done = f32[8,4096]{1,0:T(8,128)} async-done(((f32[64,4096]{1,0:T(8,128)}), f32[8,4096]{1,0:T(8,128)}) %reduce-scatter.6.cloned.1.call-update) | async-done | bytes 131088 | tf_op jit(solution)/shard_map/reduce_scatter | solution.py:91
  135.5 1.1 multiply_reduce_fusion
  136.6 1.0 multiply_convert_fusion
  137.6 0.9 broadcast_select_fusion
  138.5 3.5 all-to-all-start.1
  142.5 9.8 %all-to-all-done.1 = bf16[8,8,4096]{2,1,0:T(8,128)(2,1)S(1)} async-done(((bf16[8,8,4096]{2,1,0:T(8,128)(2,1)}), bf16[8,8,4096]{2,1,0:T(8,128)(2,1)S(1)}, u32[]{:S(2)}, u32[]{:S(2)}) %all-to-all-start.1) | async-done | bytes 524320 | tf_op jit(solution)/shard_map/all_to_all | solution.py:106
  152.2 0.9 fusion.5
  153.4 86.4 %all-gather.5.cloned.1.call-done = bf16[768,1,4096]{2,0,1:T(8,128)(2,1)} async-done(((bf16[24,1,4096]{2,0,1:T(8,128)(2,1)}), bf16[768,1,4096]{2,0,1:T(8,128)(2,1)}) %all-gather.5.cloned.1.call-update) | async-done | bytes 6291472 | tf_op jit(solution)/shard_map/all_gather | solution.py:122
  239.8 6.9 %fusion.9 = f32[768,1,448]{0,2,1:T(8,128)S(1)} fusion(bf16[1,4096,448]{1,2,0:T(8,128)(2,1)} %param.26, bf16[768,1,4096]{2,0,1:T(8,128)(2,1)} %all-gather.5.cloned.1.call-done), kind=kOutput, calls=%fused_computation.13 | convolution fusion | flops 2818572288 | bytes 11337728 | tf_op jit(solution)/shard_map/ned,edf->nef/dot_general | solution.py:53
  246.7 17.8 %convolution_bitcast_fusion = f32[768,1,4096]{2,0,1:T(8,128)} fusion(bf16[1,448,4096]{2,1,0:T(8,128)(2,1)} %param.28, bf16[1,4096,448]{1,2,0:T(8,128)(2,1)} %param.27, bf16[768,1,4096]{2,0,1:T(8,128)(2,1)} %all-gather.5.cloned.1.call-done, f32[768,1,448]{0,2,1:T(8,128)S(1)} %fusion.9), kind=kOutput, calls=%fused_computation.1 | convolution fusion | flops 5639208960 | bytes 27590656 | tf_op jit(solution)/shard_map/nef,efd->ned/dot_general | solution.py:56
  264.6 236.8 %reduce-scatter.8.cloned.1.call-done = f32[24,1,4096]{2,0,1:T(8,128)} async-done(((f32[768,1,4096]{2,0,1:T(8,128)}), f32[24,1,4096]{2,0,1:T(8,128)}) %reduce-scatter.8.cloned.1.call-update) | async-done | bytes 393232 | tf_op jit(solution)/shard_map/reduce_scatter | solution.py:123
  501.4 1.6 convolution_bitcast_fusion.2
  503.0 2.1 copy.45
  505.1 4.3 all-to-all-start.2
  509.9 15.4 %all-to-all-done.2 = f32[1,64,4096]{2,0,1:T(1,128)S(1)} async-done(((f32[1,64,4096]{2,0,1:T(1,128)}), f32[1,64,4096]{2,0,1:T(1,128)S(1)}, u32[]{:S(2)}, u32[]{:S(2)}) %all-to-all-start.2) | async-done | bytes 1048608 | tf_op jit(solution)/shard_map/all_to_all | solution.py:129
  525.3 0.6 copy.86
  525.9 1.5 fusion.47
  527.4 3.2 convolution_bitcast_fusion.1
  530.7 34.0 %reduce-scatter.10.cloned.1.call-done = f32[512,2]{1,0:T(8,128)} async-done(((f32[4096,2]{1,0:T(8,128)}), f32[512,2]{1,0:T(8,128)}) %reduce-scatter.10.cloned.1.call-update) | async-done | bytes 4112
  564.6 1.1 copy.58
  565.9 12.9 %psum.7 = f32[2]{0:T(128)S(1)} all-reduce(f32[2]{0:T(128)S(1)} %multiply_reduce_fusion.1), channel_id=1, replica_groups=mesh['dp'=32,'expert'=8] {'expert'}, use_global_device_ids=true, to_apply=%region_12.13 | all-reduce | flops 2 | bytes 16 | tf_op jit(solution)/shard_map/psum | solution.py:137
  579.2 0.7 all_to_all.34
  579.8 10.2 %all-to-all-start.3 = ((bf16[32,2,512]{2,1,0:T(2,128)(2,1)}), bf16[32,2,512]{2,1,0:T(2,128)(2,1)S(1)}, u32[]{:S(2)}, u32[]{:S(2)}) async-start(bf16[32,2,512]{2,1,0:T(2,128)(2,1)} %all_to_all.34), calls=%async_computation.5 | async-start | bytes 131072 | tf_op jit(solution)/shard_map/all_to_all | solution.py:142
  590.1 8.7 %all-to-all-done.3 = bf16[32,2,512]{2,1,0:T(2,128)(2,1)S(1)} async-done(((bf16[32,2,512]{2,1,0:T(2,128)(2,1)}), bf16[32,2,512]{2,1,0:T(2,128)(2,1)S(1)}, u32[]{:S(2)}, u32[]{:S(2)}) %all-to-all-start.3) | async-done | bytes 65568 | tf_op jit(solution)/shard_map/all_to_all | solution.py:142
  599.1 0.8 fusion.46
  (64 shorter events, 4.2 us)
Async XLA Ops:
  7.2 1.7 copy-start
  7.2 4.3 copy-start.8
  7.2 89.3 %all-gather.3.cloned.1.call-start = ((), (), s32[]{:S(2)}) async-start(), calls=%async_computation.7 | async-start | bytes 4325376 | tf_op jit(solution)/shard_map/all_gather | solution.py:88
  7.9 127.6 %reduce-scatter.6.cloned.1.call-start = ((), (), s32[]{:S(2)}) async-start(), calls=%async_computation.8 | async-start | bytes 1179648 | tf_op jit(solution)/shard_map/reduce_scatter | solution.py:91
  11.9 88.6 %copy-start.7 = (s32[8,2]{0,1:T(2,128)S(1)}, s32[8,2]{0,1:T(2,128)}, u32[]{:S(2)}) copy-start(s32[8,2]{0,1:T(2,128)} %param.25) | copy-start | bytes 196
  11.9 123.6 %copy-start.3 = (bf16[8,4096]{1,0:T(8,128)(2,1)S(1)}, bf16[8,4096]{1,0:T(8,128)(2,1)}, u32[]{:S(2)}) copy-start(bf16[8,4096]{1,0:T(8,128)(2,1)} %param.16) | copy-start | bytes 196612
  11.9 124.7 %copy-start.5 = (f32[4096]{0:T(1024)S(1)}, f32[4096]{0:T(1024)}, u32[]{:S(2)}) copy-start(f32[4096]{0:T(1024)} %param.23) | copy-start | bytes 49156
  101.1 37.4 %all-to-all-start = ((s32[8,1,8]{2,1,0:T(1,128)}), s32[8,1,8]{2,1,0:T(1,128)S(1)}, u32[]{:S(2)}, u32[]{:S(2)}) async-start(s32[8,1,8]{2,1,0:T(1,128)} %compare_select_fusion.1), calls=%async_computation.1 | async-start | bytes 8192 | tf_op jit(solution)/shard_map/all_to_all | solution.py:107
  138.5 13.7 %all-to-all-start.1 = ((bf16[8,8,4096]{2,1,0:T(8,128)(2,1)}), bf16[8,8,4096]{2,1,0:T(8,128)(2,1)S(1)}, u32[]{:S(2)}, u32[]{:S(2)}) async-start(bf16[8,8,4096]{2,1,0:T(8,128)(2,1)} %broadcast_select_fusion), calls=%async_computation.2 | async-start | bytes 1048576 | tf_op jit(solution)/shard_map/all_to_all | solution.py:106
  142.0 97.8 %all-gather.5.cloned.1.call-start = ((), (), s32[]{:S(2)}) async-start(), calls=%async_computation.9 | async-start | bytes 6488064 | tf_op jit(solution)/shard_map/all_gather | solution.py:122
  153.1 348.2 %reduce-scatter.8.cloned.1.call-start = ((), (), s32[]{:S(2)}) async-start(), calls=%async_computation.10 | async-start | bytes 12976128 | tf_op jit(solution)/shard_map/reduce_scatter | solution.py:123
  264.5 245.1 %copy-start.4 = (bf16[4096,8]{0,1:T(8,128)(2,1)S(1)}, bf16[4096,8]{0,1:T(8,128)(2,1)}, u32[]{:S(2)}) copy-start(bf16[4096,8]{0,1:T(8,128)(2,1)} %param.24) | copy-start | bytes 196612
  503.0 24.4 %copy-start.2 = (f32[8,4096]{1,0:T(8,128)S(1)}, f32[8,4096]{1,0:T(8,128)}, u32[]{:S(2)}) copy-start(f32[8,4096]{1,0:T(8,128)} %reduce-scatter.6.cloned.1.call-done) | copy-start | bytes 393220
  505.1 20.2 %all-to-all-start.2 = ((f32[1,64,4096]{2,0,1:T(1,128)}), f32[1,64,4096]{2,0,1:T(1,128)S(1)}, u32[]{:S(2)}, u32[]{:S(2)}) async-start(f32[1,64,4096]{2,0,1:T(1,128)} %copy.45), calls=%async_computation.4 | async-start | bytes 2097152 | tf_op jit(solution)/shard_map/all_to_all | solution.py:129
  509.3 55.3 %reduce-scatter.10.cloned.1.call-start = ((), (), s32[]{:S(2)}) async-start(), calls=%async_computation.11 | async-start | bytes 2359296
  509.9 20.7 %copy-start.9 = (s32[64]{0:T(128)S(1)}, s32[64]{0:T(128)}, u32[]{:S(2)}) copy-start(s32[64]{0:T(128)} %param.31) | copy-start | bytes 772
  509.9 68.9 %copy-start.6 = (f32[512]{0:T(512)S(1)}, f32[512]{0:T(512)}, u32[]{:S(2)}) copy-start(f32[512]{0:T(512)} %param.29) | copy-start | bytes 6148
  525.9 64.2 %copy-start.10 = (f32[4]{0:T(128)S(1)}, f32[4]{0:T(128)}, u32[]{:S(2)}) copy-start(f32[4]{0:T(128)} %param.30) | copy-start | bytes 52
  578.9 21.0 %copy-start.1 = (bf16[2,512]{1,0:T(2,128)(2,1)}, bf16[2,512]{1,0:T(2,128)(2,1)S(1)}, u32[]{:S(2)}) copy-start(bf16[2,512]{1,0:T(2,128)(2,1)S(1)} %multiply_convert_fusion.1) | copy-start | bytes 6148
  579.8 18.9 %all-to-all-start.3 = ((bf16[32,2,512]{2,1,0:T(2,128)(2,1)}), bf16[32,2,512]{2,1,0:T(2,128)(2,1)S(1)}, u32[]{:S(2)}, u32[]{:S(2)}) async-start(bf16[32,2,512]{2,1,0:T(2,128)(2,1)} %all_to_all.34), calls=%async_computation.5 | async-start | bytes 131072 | tf_op jit(solution)/shard_map/all_to_all | solution.py:142
Sparse Core Ops, SparseCore 0:
  10.5 85.9 all-gather.2
  100.6 34.8 reduce-scatter.5
  153.3 86.4 all-gather.4
  264.7 236.6 reduce-scatter.7
  530.7 33.8 reduce-scatter.9
